TPU v7x, 32 devices: a whole 2x2x4 slice. The times are simulated.
32 devices in a mesh: patch: 8 (over z, y), band: 4 (over x, core).
Axes of the slice: x: 2, y: 2, z: 4, core: 2. Of those that a mesh axis runs over, the one named last changes fastest.
Arguments:
- exposures: float32 [64, 256, 128], P(('band', 'patch')), parts along dimension 0, may hold values from -6 to 6
- variance: float32 [64, 256, 128], P(('band', 'patch')), parts along dimension 0, may hold values from 0.01 to 60, as said below
- mask_bits: int32 [64, 256, 128], P(('band', 'patch')), parts along dimension 0, may hold values from 0 to 4095
- kernel_coeffs: float32 [64, 27, 6], P(('band', 'patch')), parts along dimension 0, may hold values from -3 to 3
- ccd_visit: int32 [64, 1], P(('band', 'patch')), parts along dimension 0, may hold values from 0 to 7
- strip_patch: int32 [2048, 1], P(('band', 'patch')), parts along dimension 0, may hold values from 0 to 7, as said below
- strip_row: int32 [2048], P(('band', 'patch')), parts along dimension 0, may hold values from 0 to 120
- strip_col: int32 [2048], P(('band', 'patch')), parts along dimension 0, may hold values from 0 to 384
Outputs:
- coadd_image: float32 [32, 128, 512], P(('band', 'patch')), parts along dimension 0
- weight_map: float32 [32, 128, 512], P(('band', 'patch')), parts along dimension 0
There are 4 independent parts, one for each index of `band`. A program takes and returns all parts, laid end to end along the dimension named above; each array names one. Nothing has to cross between parts.
Inputs may be any that keep to these rules, and one draw needn't show every extreme that they name: `variance`: Positive. `ccd_visit`: every visit has at least one CCD. `strip_patch`: among the strips of one device (aligned blocks of 64 rows) no patch is named more than 16 times; one patch is named exactly 16 times in every block.
All inputs are finite; a program needn't handle non-finite values.
Results may differ from a plain program's by a relative error of at most 0.00011.
Values sent between devices are 32-bit elements; how exact they have to be, the bound alone decides.
No kernel may reach another device: no remote copies, remote signals or barrier semaphores. Data moves between devices by JAX's collectives and lax.ppermute only.
A program may use at most 64 MiB of HBM per device.

v0:
```python
import math
import jax
import jax.numpy as jnp
from jax import lax
from jax.sharding import PartitionSpec as P

PH = 128
PW = 512
KS = 21
VISITS = 8
gauss_widths = (0.75, 1.5, 3.0)
largest_value = lax.Precision.HIGHEST
mxu_value = lax.Precision.HIGH


def tap_values(offsets, kernel_half_width):
    support = jnp.arange(-kernel_half_width, kernel_half_width + 1).astype(jnp.float32)
    inside = (jnp.abs(offsets) <= kernel_half_width).astype(jnp.float32)
    tables = []
    for spread in gauss_widths:
        gauss_total = jnp.sum(jnp.exp(-support * support / (2.0 * spread * spread)))
        profile = jnp.exp(-offsets * offsets / (2.0 * spread * spread)) / gauss_total * inside
        scaled = offsets / spread
        tables.append(jnp.stack([profile, profile * scaled, profile * scaled * scaled]))
    return jnp.stack(tables)


def row_filters(row_count, kernel_half_width):
    row_ids = jnp.arange(row_count)[:, None]
    window_ids = jnp.arange(row_count + 2 * kernel_half_width)[None, :]
    return tap_values(
        (window_ids - row_ids - kernel_half_width).astype(jnp.float32), kernel_half_width
    )


def column_filters(column_count, kernel_half_width):
    source = jnp.arange(column_count)[:, None]
    target_patch = jnp.arange(column_count)[None, :]
    return tap_values((source - target_patch).astype(jnp.float32), kernel_half_width)


def convolve_all(padded, kernel_coeffs, height):
    kernel_half_width = KS // 2
    n, _, columns = padded.shape
    rows = row_filters(height, kernel_half_width).reshape(9, height, height + 2 * kernel_half_width)
    smooth = jnp.einsum("krj,njx->nkrx", rows, padded, precision=mxu_value)
    col_ops = column_filters(columns, kernel_half_width)
    x_line = 2.0 * jnp.arange(columns).astype(jnp.float32) / (columns - 1) - 1.0
    coef = kernel_coeffs.reshape(n, 3, 3, 3, 6)
    c = [coef[..., p, None] for p in range(6)]
    fx = jnp.stack(
        [
            c[0] + c[1] * x_line + c[3] * (x_line * x_line),
            c[2] + c[4] * x_line,
            jnp.broadcast_to(c[5], c[0].shape[:-1] + (columns,)),
        ],
        axis=4,
    )
    mixed = jnp.sum(col_ops[None, :, None, :, :, None, :] * fx[:, :, :, :, None, :, :], axis=3)
    mixed = mixed.reshape(n, 9, columns, 3 * columns)
    fields = jnp.einsum("nkry,nkyz->nrz", smooth, mixed, precision=mxu_value)
    y_line = (2.0 * jnp.arange(height).astype(jnp.float32) / (height - 1) - 1.0)[None, :, None]
    return (
        fields[:, :, :columns]
        + y_line * fields[:, :, columns : 2 * columns]
        + y_line * y_line * fields[:, :, 2 * columns :]
    )


def place_slots(flux_flat, weight_flat, offsets, patch_rows, patch_cols):
    slot_total, strip_rows, columns = flux_flat.shape
    group = math.gcd(slot_total, 16)
    pairs = jnp.stack([flux_flat, weight_flat], axis=1).reshape(
        slot_total // group, group, 2, strip_rows, columns
    )
    grouped_offsets = offsets.reshape(slot_total // group, group, offsets.shape[1])
    target_cols = jnp.arange(patch_cols)
    source_cols = jnp.arange(columns)
    target_rows = jnp.arange(patch_rows)
    source_rows = jnp.arange(strip_rows)

    def place_group(total, item):
        pixel_block_tile, block_offsets = item
        column_selection = (
            target_cols[None, None, :]
            == block_offsets[:, 1][:, None, None] + source_cols[None, :, None]
        ).astype(jnp.float32)
        row_select = (
            target_rows[None, :, None]
            == block_offsets[:, 0][:, None, None] + source_rows[None, None, :]
        ).astype(jnp.float32)
        broadened_width = jnp.einsum(
            "vmwn,vny->vmwy", pixel_block_tile, column_selection, precision=largest_value
        )
        return (
            total
            + jnp.einsum("gri,gkip->krp", row_select, broadened_width, precision=largest_value),
            None,
        )

    start = jnp.zeros((2, patch_rows, patch_cols), jnp.float32)
    placed, _ = lax.scan(place_group, start, (pairs, grouped_offsets))
    return (placed[0], placed[1])


def shards(
    exposures, variance, mask_bits, kernel_coeffs, ccd_visit, strip_patch, strip_row, strip_col
):
    ccd_count, height, columns = exposures.shape
    strip_total = strip_patch.shape[0]
    per_ccd = strip_total // ccd_count
    strip_rows = height // per_ccd
    devices = lax.axis_size("patch")
    capacity = 2 * strip_total // devices
    kernel_half_width = KS // 2
    usable = (jnp.bitwise_and(mask_bits, 3) != 3).astype(jnp.float32)
    visit_hot = (ccd_visit == jnp.arange(VISITS)[None, :]).astype(jnp.float32)
    local_count = jnp.sum(jnp.sum(usable, axis=(1, 2))[:, None] * visit_hot, axis=0)
    local_load = jnp.sum(jnp.sum(usable * variance, axis=(1, 2))[:, None] * visit_hot, axis=0)
    destination = strip_patch[:, 0]
    strip_ids = jnp.arange(strip_total)
    earlier = strip_ids[None, :] < strip_ids[:, None]
    same_target = destination[None, :] == destination[:, None]
    slot_rank = jnp.sum(jnp.logical_and(earlier, same_target).astype(jnp.int32), axis=1)
    slot_index = destination * capacity + slot_rank
    slot_total = devices * capacity
    chooser = (slot_index[None, :] == jnp.arange(slot_total)[:, None]).astype(jnp.float32)
    padded = jnp.pad(exposures, ((0, 0), (kernel_half_width, kernel_half_width), (0, 0)))
    convolved = convolve_all(padded, kernel_coeffs, height)
    tiles = jnp.concatenate(
        [
            (usable * convolved).reshape(strip_total, strip_rows, columns),
            usable.reshape(strip_total, strip_rows, columns),
        ],
        axis=1,
    ).reshape(strip_total, 2 * strip_rows * columns)
    packed = jnp.dot(chooser, tiles, precision=largest_value).reshape(
        devices, capacity * 2 * strip_rows, columns
    )
    strip_visit = jnp.repeat(ccd_visit[:, 0], per_ccd)
    placement = jnp.stack([strip_row, strip_col, strip_visit], axis=1).astype(jnp.float32)
    slot_meta = jnp.dot(chooser, placement, precision=largest_value).reshape(devices, capacity, 3)
    meta = jnp.zeros((devices, 8, columns), jnp.float32)
    meta = meta.at[:, 0:3, :capacity].set(jnp.swapaxes(slot_meta, 1, 2))
    meta = meta.at[:, 3, :VISITS].set(jnp.broadcast_to(local_count, (devices, VISITS)))
    meta = meta.at[:, 4, :VISITS].set(jnp.broadcast_to(local_load, (devices, VISITS)))
    payload = jnp.concatenate([packed, meta], axis=1)
    got = lax.all_to_all(payload, "patch", split_axis=0, concat_axis=0, tiled=True)
    body_rows = capacity * 2 * strip_rows
    got_meta = got[:, body_rows:, :]
    visit_count = jnp.sum(got_meta[:, 3, :VISITS], axis=0)
    visit_load = jnp.sum(got_meta[:, 4, :VISITS], axis=0)
    visit_weight = (visit_count + 1.0) / (visit_load + 1.0)
    slot_rows = got_meta[:, 0, :capacity].reshape(slot_total).astype(jnp.int32)
    slot_cols = got_meta[:, 1, :capacity].reshape(slot_total).astype(jnp.int32)
    slot_visit = got_meta[:, 2, :capacity].reshape(slot_total).astype(jnp.int32)
    slot_hot = (slot_visit[:, None] == jnp.arange(VISITS)[None, :]).astype(jnp.float32)
    slot_weight = jnp.sum(slot_hot * visit_weight[None, :], axis=1)
    body = got[:, :body_rows, :].reshape(slot_total, 2, strip_rows, columns)
    body = body * slot_weight[:, None, None, None]
    offsets = jnp.stack([slot_rows, slot_cols], axis=1)
    numerator, weight_map = place_slots(body[:, 0], body[:, 1], offsets, PH, PW)
    coadd_image = numerator / jnp.maximum(weight_map, 1.0)
    return (coadd_image[None], weight_map[None])


def solution(mesh):
    return jax.shard_map(
        shards,
        mesh=mesh,
        in_specs=(
            P(("band", "patch"), None, None),
            P(("band", "patch"), None, None),
            P(("band", "patch"), None, None),
            P(("band", "patch"), None, None),
            P(("band", "patch"), None),
            P(("band", "patch"), None),
            P(("band", "patch")),
            P(("band", "patch")),
        ),
        out_specs=(P(("band", "patch"), None, None), P(("band", "patch"), None, None)),
        check_vma=False,
    )
```

profile of v0, /device:TPU:0, one launch (start us, length us, event | category | flops | bytes accessed | tf_op | source)
XLA Modules:
  0.0 92.9 jit_solution(15024950080672934833)
XLA Ops:
  0.7 0.7 exponential_reduce_fusion.2
  1.3 0.7 divide_select_fusion.5
  2.1 0.7 fusion.40
  2.8 0.6 exponential_reduce_fusion.1
  3.4 0.7 divide_select_fusion.4
  4.1 0.7 fusion.42
  4.8 0.6 exponential_reduce_fusion
  5.4 0.7 divide_select_fusion.3
  6.1 0.7 fusion.38
  6.8 1.6 %divide_select_fusion.2 = (f32[1,256,276]{1,2,0:T(8,128)}, f32[1,256,276]{1,2,0:T(8,128)}) fusion(f32[]{:T(128)} %exponential_reduce_fusion.2), kind=kLoop, calls=%fused_computation.40 | loop fusion | flops 918528 | bytes 565252 | tf_op jit(solution)/shard_map/mul | solution.py:22
  8.5 1.5 %fusion.30 = f32[1,256,276]{1,2,0:T(8,128)} fusion(f32[]{:T(128)} %exponential_reduce_fusion.2), kind=kLoop, calls=%fused_computation.49 | loop fusion | flops 847872 | bytes 282628 | tf_op jit(solution)/shard_map/mul | solution.py:24
  10.0 1.6 %divide_select_fusion.1 = (f32[1,256,276]{1,2,0:T(8,128)}, f32[1,256,276]{1,2,0:T(8,128)}) fusion(f32[]{:T(128)} %exponential_reduce_fusion.1), kind=kLoop, calls=%fused_computation.39 | loop fusion | flops 918528 | bytes 565252 | tf_op jit(solution)/shard_map/mul | solution.py:22
  11.6 1.5 %fusion.32 = f32[1,256,276]{1,2,0:T(8,128)} fusion(f32[]{:T(128)} %exponential_reduce_fusion.1), kind=kLoop, calls=%fused_computation.51 | loop fusion | flops 847872 | bytes 282628 | tf_op jit(solution)/shard_map/mul | solution.py:24
  13.1 1.6 %divide_select_fusion = (f32[1,256,276]{1,2,0:T(8,128)}, f32[1,256,276]{1,2,0:T(8,128)}) fusion(f32[]{:T(128)} %exponential_reduce_fusion), kind=kLoop, calls=%fused_computation.38 | loop fusion | flops 918528 | bytes 565252 | tf_op jit(solution)/shard_map/mul | solution.py:22
  14.7 1.5 %fusion.28 = f32[1,256,276]{1,2,0:T(8,128)} fusion(f32[]{:T(128)} %exponential_reduce_fusion), kind=kLoop, calls=%fused_computation.47 | loop fusion | flops 847872 | bytes 282628 | tf_op jit(solution)/shard_map/mul | solution.py:24
  16.2 0.1 copy.68
  16.3 0.2 fusion.57
  16.5 0.2 copy.69
  16.8 0.2 copy.71
  17.0 0.2 copy.73
  17.2 0.2 copy.75
  17.5 0.2 copy.77
  17.7 0.2 copy.79
  17.9 0.4 multiply_add_fusion.1
  18.3 0.1 stack_broadcast_in_dim.2
  18.6 2.7 %multiply_reduce_fusion = f32[2,3,3,128,3,128]{5,3,4,2,1,0:T(8,128)} fusion(f32[2,3,3,3,3,128]{5,4,3,2,1,0:T(4,128)S(1)} %pad_maximum_fusion.4, f32[3,3,128,128]{3,2,1,0:T(8,128)S(1)} %pad_maximum_fusion.2), kind=kLoop, calls=%fused_computation.20 | loop fusion | flops 4423680 | bytes 4211712 | tf_op jit(solution)/shard_map/reduce_sum | solution.py:59
  21.3 3.3 %copy.81 = f32[2,3,3,128,3,128]{3,5,4,2,1,0:T(8,128)S(1)} copy(f32[2,3,3,128,3,128]{5,3,4,2,1,0:T(8,128)} %multiply_reduce_fusion) | data formatting | bytes 7077888 | tf_op jit(solution)/shard_map/reduce_sum | solution.py:59
  24.7 1.3 %maximum_bitcast_fusion = f32[1,3,256,276]{2,3,1,0:T(8,128)S(1)} fusion(f32[1,256,276]{1,2,0:T(8,128)} %get-tuple-element.195, f32[1,256,276]{1,2,0:T(8,128)} %fusion.30, f32[1,256,276]{1,2,0:T(8,128)} %get-tuple-element.194), kind=kLoop, calls=%fused_computation.26 | loop fusion | flops 423936 | bytes 1695744 | tf_op jit(solution)/shard_map/stack | solution.py:25
  26.0 1.2 %maximum_bitcast_fusion.1 = f32[1,3,256,276]{2,3,1,0:T(8,128)S(1)} fusion(f32[1,256,276]{1,2,0:T(8,128)} %get-tuple-element.191, f32[1,256,276]{1,2,0:T(8,128)} %fusion.32, f32[1,256,276]{1,2,0:T(8,128)} %get-tuple-element.190), kind=kLoop, calls=%fused_computation.27 | loop fusion | flops 423936 | bytes 1695744 | tf_op jit(solution)/shard_map/stack | solution.py:25
  27.3 0.2 pad_maximum_fusion
  27.5 0.7 copy-done.3
  28.2 2.2 %fusion.25 = f32[2,128,9,256]{3,1,2,0:T(8,128)S(1)} fusion(f32[9,256,276,1]{1,2,0,3:T(8,128)S(1)} %bitcast.103, f32[2,256,128]{2,1,0:T(8,128)S(1)} %copy-done.3), kind=kOutput, calls=%fused_computation.36 | convolution fusion | flops 976748544 | bytes 5165056 | tf_op jit(solution)/shard_map/krj,njx->nkrx/dot_general | solution.py:46
  30.5 4.1 %fusion.19 = f32[2,256,384]{2,1,0:T(8,128)S(1)} fusion(f32[2,9,128,384]{2,3,1,0:T(8,128)S(1)} %bitcast.102, f32[2,128,9,256]{3,1,2,0:T(8,128)S(1)} %fusion.25), kind=kOutput, calls=%fused_computation.24 | convolution fusion | flops 1358954496 | bytes 6684672 | tf_op jit(solution)/shard_map/nkry,nkyz->nrz/dot_general | solution.py:61
  34.6 0.1 fusion.35
  34.8 0.2 convert_reduce_fusion.1
  35.1 0.7 fusion.22
  35.8 0.2 reshape.602
  36.0 0.2 select_reduce_fusion
  36.3 0.1 fusion.43
  36.7 0.3 scatter.11
  37.0 0.4 scatter.14
  37.4 1.1 %pad_maximum_fusion.1 = f32[8,264,128]{2,1,0:T(8,128)} fusion(f32[8,8,128]{2,1,0:T(8,128)S(1)} %scatter.14, f32[8,256,128]{2,1,0:T(8,128)S(1)} %reshape.602), kind=kLoop, calls=%fused_computation.25 | loop fusion | flops 270336 | bytes 2162688 | tf_op jit(solution)/shard_map/concatenate | solution.py:147
  38.5 7.3 %all-to-all-start = ((f32[8,264,128]{2,1,0:T(8,128)}), f32[8,264,128]{2,1,0:T(8,128)S(1)}, u32[]{:S(2)}, u32[]{:S(2)}) async-start(f32[8,264,128]{2,1,0:T(8,128)} %pad_maximum_fusion.1), calls=%async_computation | async-start | bytes 2162688 | tf_op jit(solution)/shard_map/all_to_all | solution.py:148
  45.8 26.5 %all-to-all-done = f32[8,264,128]{2,1,0:T(8,128)S(1)} async-done(((f32[8,264,128]{2,1,0:T(8,128)}), f32[8,264,128]{2,1,0:T(8,128)S(1)}, u32[]{:S(2)}, u32[]{:S(2)}) %all-to-all-start) | async-done | bytes 1081376 | tf_op jit(solution)/shard_map/all_to_all | solution.py:148
  72.7 0.2 broadcast_multiply_fusion
  72.9 19.0 %while.16 = (s32[]{:T(128)}, f32[2,128,512]{1,2,0:T(8,128)S(1)}, f32[8,16,2,8,128]{4,3,2,1,0:T(8,128)S(1)}, s32[8,16,2]{1,0,2:T(8,128)S(1)}, s32[]{:T(128)}, /*index=5*/s32[]{:T(128)}) while((s32[]{:T(128)}, f32[2,128,512]{1,2,0:T(8,128)S(1)}, f32[8,16,2,8,128]{4,3,2,1,0:T(8,128)S(1)}, s32[8,16,2]{1,0,2:T(8,128)S(1)}, ...), condition=%wide.region_13.14_spmd.clone.clone, body=%wide.region_12.13_spmd.clone.clone.sunk | while | flops 403982464 | bytes 2246359 | solution.py:102
  73.0 1.5 %fusion.71 = f32[16,2,8,512]{3,2,1,0:T(8,128)S(1)} fusion(s32[16,128]{1,0:T(8,128)S(1)} %iota_add_fusion.4, f32[8,16,2,8,128]{4,3,2,1,0:T(8,128)S(1)} %get-tuple-element.243, s32[]{:T(128)} %get-tuple-element.235), kind=kOutput, calls=%fused_computation.5.clone.1 | convolution fusion | flops 202375168 | bytes 663556 | tf_op jit(solution)/shard_map/while/body/eval_jaxpr/vmwn,vny->vmwy/dot_general | solution.py:92
  74.6 0.7 fusion.72
  75.4 1.5 %fusion.71 = f32[16,2,8,512]{3,2,1,0:T(8,128)S(1)} fusion(s32[16,128]{1,0:T(8,128)S(1)} %iota_add_fusion.4, f32[8,16,2,8,128]{4,3,2,1,0:T(8,128)S(1)} %get-tuple-element.243, s32[]{:T(128)} %get-tuple-element.235), kind=kOutput, calls=%fused_computation.5.clone.1 | convolution fusion | flops 202375168 | bytes 663556 | tf_op jit(solution)/shard_map/while/body/eval_jaxpr/vmwn,vny->vmwy/dot_general | solution.py:92
  76.9 0.7 fusion.72
  77.8 1.5 %fusion.71 = f32[16,2,8,512]{3,2,1,0:T(8,128)S(1)} fusion(s32[16,128]{1,0:T(8,128)S(1)} %iota_add_fusion.4, f32[8,16,2,8,128]{4,3,2,1,0:T(8,128)S(1)} %get-tuple-element.243, s32[]{:T(128)} %get-tuple-element.235), kind=kOutput, calls=%fused_computation.5.clone.1 | convolution fusion | flops 202375168 | bytes 663556 | tf_op jit(solution)/shard_map/while/body/eval_jaxpr/vmwn,vny->vmwy/dot_general | solution.py:92
  79.3 0.7 fusion.72
  80.1 1.5 %fusion.71 = f32[16,2,8,512]{3,2,1,0:T(8,128)S(1)} fusion(s32[16,128]{1,0:T(8,128)S(1)} %iota_add_fusion.4, f32[8,16,2,8,128]{4,3,2,1,0:T(8,128)S(1)} %get-tuple-element.243, s32[]{:T(128)} %get-tuple-element.235), kind=kOutput, calls=%fused_computation.5.clone.1 | convolution fusion | flops 202375168 | bytes 663556 | tf_op jit(solution)/shard_map/while/body/eval_jaxpr/vmwn,vny->vmwy/dot_general | solution.py:92
  81.7 0.7 fusion.72
  82.5 1.5 %fusion.71 = f32[16,2,8,512]{3,2,1,0:T(8,128)S(1)} fusion(s32[16,128]{1,0:T(8,128)S(1)} %iota_add_fusion.4, f32[8,16,2,8,128]{4,3,2,1,0:T(8,128)S(1)} %get-tuple-element.243, s32[]{:T(128)} %get-tuple-element.235), kind=kOutput, calls=%fused_computation.5.clone.1 | convolution fusion | flops 202375168 | bytes 663556 | tf_op jit(solution)/shard_map/while/body/eval_jaxpr/vmwn,vny->vmwy/dot_general | solution.py:92
  84.0 0.7 fusion.72
  84.9 1.5 %fusion.71 = f32[16,2,8,512]{3,2,1,0:T(8,128)S(1)} fusion(s32[16,128]{1,0:T(8,128)S(1)} %iota_add_fusion.4, f32[8,16,2,8,128]{4,3,2,1,0:T(8,128)S(1)} %get-tuple-element.243, s32[]{:T(128)} %get-tuple-element.235), kind=kOutput, calls=%fused_computation.5.clone.1 | convolution fusion | flops 202375168 | bytes 663556 | tf_op jit(solution)/shard_map/while/body/eval_jaxpr/vmwn,vny->vmwy/dot_general | solution.py:92
  86.4 0.7 fusion.72
  87.3 1.5 %fusion.71 = f32[16,2,8,512]{3,2,1,0:T(8,128)S(1)} fusion(s32[16,128]{1,0:T(8,128)S(1)} %iota_add_fusion.4, f32[8,16,2,8,128]{4,3,2,1,0:T(8,128)S(1)} %get-tuple-element.243, s32[]{:T(128)} %get-tuple-element.235), kind=kOutput, calls=%fused_computation.5.clone.1 | convolution fusion | flops 202375168 | bytes 663556 | tf_op jit(solution)/shard_map/while/body/eval_jaxpr/vmwn,vny->vmwy/dot_general | solution.py:92
  88.8 0.7 fusion.72
  89.6 1.5 %fusion.71 = f32[16,2,8,512]{3,2,1,0:T(8,128)S(1)} fusion(s32[16,128]{1,0:T(8,128)S(1)} %iota_add_fusion.4, f32[8,16,2,8,128]{4,3,2,1,0:T(8,128)S(1)} %get-tuple-element.243, s32[]{:T(128)} %get-tuple-element.235), kind=kOutput, calls=%fused_computation.5.clone.1 | convolution fusion | flops 202375168 | bytes 663556 | tf_op jit(solution)/shard_map/while/body/eval_jaxpr/vmwn,vny->vmwy/dot_general | solution.py:92
  91.2 0.7 fusion.72
  91.9 0.2 copy.88
  92.1 0.8 slice_divide_fusion
  (90 shorter events, 2.4 us)
Async XLA Ops:
  0.6 15.6 %copy-start.6 = (f32[2,27,6]{1,0,2:T(2,128)S(1)}, f32[2,27,6]{1,0,2:T(2,128)}, u32[]{:S(2)}) copy-start(f32[2,27,6]{1,0,2:T(2,128)} %param.19) | copy-start | bytes 3892
  24.6 2.5 %copy-start = (f32[1,256,276]{1,2,0:T(8,128)S(1)}, f32[1,256,276]{1,2,0:T(8,128)}, u32[]{:S(2)}) copy-start(f32[1,256,276]{1,2,0:T(8,128)} %fusion.28) | copy-start | bytes 847876
  24.7 2.5 %copy-start.1 = (f32[1,256,276]{1,2,0:T(8,128)S(1)}, f32[1,256,276]{1,2,0:T(8,128)}, u32[]{:S(2)}) copy-start(f32[1,256,276]{1,2,0:T(8,128)} %get-tuple-element.186) | copy-start | bytes 847876
  24.7 2.5 %copy-start.2 = (f32[1,256,276]{1,2,0:T(8,128)S(1)}, f32[1,256,276]{1,2,0:T(8,128)}, u32[]{:S(2)}) copy-start(f32[1,256,276]{1,2,0:T(8,128)} %get-tuple-element.187) | copy-start | bytes 847876
  27.3 1.0 %copy-start.3 = (f32[2,256,128]{2,1,0:T(8,128)S(1)}, f32[2,256,128]{2,1,0:T(8,128)}, u32[]{:S(2)}) copy-start(f32[2,256,128]{2,1,0:T(8,128)} %param.16) | copy-start | bytes 786436
  30.5 4.1 %copy-start.5 = (s32[2,256,128]{2,1,0:T(8,128)S(1)}, s32[2,256,128]{2,1,0:T(8,128)}, u32[]{:S(2)}) copy-start(s32[2,256,128]{2,1,0:T(8,128)} %param.18) | copy-start | bytes 786436
  30.5 4.3 %copy-start.8 = (s32[64,1]{0,1:T(1,128)S(1)}, s32[64,1]{0,1:T(1,128)}, u32[]{:S(2)}) copy-start(s32[64,1]{0,1:T(1,128)} %param.21) | copy-start | bytes 772
  34.7 1.2 %copy-start.4 = (f32[2,256,128]{2,1,0:T(8,128)S(1)}, f32[2,256,128]{2,1,0:T(8,128)}, u32[]{:S(2)}) copy-start(f32[2,256,128]{2,1,0:T(8,128)} %param.17) | copy-start | bytes 786436
  34.8 1.4 %copy-start.7 = (s32[2,1]{0,1:T(1,128)S(1)}, s32[2,1]{0,1:T(1,128)}, u32[]{:S(2)}) copy-start(s32[2,1]{0,1:T(1,128)} %param.20) | copy-start | bytes 28
  34.8 1.5 %copy-start.9 = (s32[64]{0:T(128)S(1)}, s32[64]{0:T(128)}, u32[]{:S(2)}) copy-start(s32[64]{0:T(128)} %param.23) | copy-start | bytes 772
  34.8 1.5 %copy-start.10 = (s32[64]{0:T(128)S(1)}, s32[64]{0:T(128)}, u32[]{:S(2)}) copy-start(s32[64]{0:T(128)} %param.22) | copy-start | bytes 772
  38.5 33.8 %all-to-all-start = ((f32[8,264,128]{2,1,0:T(8,128)}), f32[8,264,128]{2,1,0:T(8,128)S(1)}, u32[]{:S(2)}, u32[]{:S(2)}) async-start(f32[8,264,128]{2,1,0:T(8,128)} %pad_maximum_fusion.1), calls=%async_computation | async-start | bytes 2162688 | tf_op jit(solution)/shard_map/all_to_all | solution.py:148
where the time goes:
time: 93.3 us; the launch traced here: 92.9 us
  waiting for transfers between devices  26.5 us (28%)
  other arithmetic  25.6 us (27%)
  matrix products  24.6 us (26%)
  local copies, waits for them, and re-layouts  7.52 us (8%)
  starting transfers between devices  7.31 us (8%)
  between operations  1.13 us (1%)
    all_to_all x1, waiting for transfers between devices, shards(): lax.all_to_all(payload, 'patch', split_axis=0, concat_axis=0, tiled=True)  26.5 us
    dot_general x8, matrix products, place_group(): jnp.einsum('vmwn,vny->vmwy', pixel_block_tile, column_selection, precisio...  11.7 us
    all_to_all x1, starting transfers between devices, shards(): lax.all_to_all(payload, 'patch', split_axis=0, concat_axis=0, tiled=True)  7.31 us
    mul x6, other arithmetic, tap_values(): jnp.exp(-offsets * offsets / (2.0 * spread * spread)) / gauss_total * inside  6.97 us
    mul x6, other arithmetic, tap_values(): profile * scaled  6.63 us
    dot_general x8, matrix products, place_group(): jnp.einsum('gri,gkip->krp', row_select, broadened_width, precision=larges...  5.76 us
    dot_general x1, matrix products, convolve_all(): fields = jnp.einsum('nkry,nkyz->nrz', smooth, mixed, precision=mxu_value)  4.08 us
    reduce_sum x1, local copies, waits for them, and re-layouts, convolve_all(): jnp.sum(col_ops[None, :, None, :, :, None, :] * fx[:, :, :, :, None, :, :...  3.31 us
  transfers between devices with their start and end apart: 1, of which 1 were waited for; matrix products, arithmetic and copies ran while one was open for 0% of the time, Pallas kernels for 0%

commit v1 on v0

--- a/solution.py
+++ b/solution.py
@@ -11,6 +11,28 @@
 gauss_widths = (0.75, 1.5, 3.0)
 largest_value = lax.Precision.HIGHEST
 mxu_value = lax.Precision.HIGH
+
+
+def split_up(x, dim, devices):
+    before, after = (x.shape[:dim], x.shape[dim + 1 :])
+    return jnp.moveaxis(x.reshape(*before, devices, -1, *after), dim, 0)
+
+
+def joined_along(blocks, dim):
+    shape = list(blocks.shape[1:])
+    shape[dim] *= blocks.shape[0]
+    return jnp.moveaxis(blocks, 0, dim).reshape(shape)
+
+
+def sent_to_each(value, axis, split_dim, concat_dim):
+    size, index = (lax.axis_size(axis), lax.axis_index(axis))
+    blocks = split_up(value, split_dim, size)
+    outs = [blocks[index]]
+    for step in range(1, size):
+        sent = blocks[(index + step) % size]
+        outs.append(lax.ppermute(sent, axis, [(i, (i + step) % size) for i in range(size)]))
+    blocks = jnp.stack(outs)[(index - jnp.arange(size)) % size]
+    return joined_along(blocks, concat_dim)
 
 
 def tap_values(offsets, kernel_half_width):
@@ -145,7 +167,7 @@
     meta = meta.at[:, 3, :VISITS].set(jnp.broadcast_to(local_count, (devices, VISITS)))
     meta = meta.at[:, 4, :VISITS].set(jnp.broadcast_to(local_load, (devices, VISITS)))
     payload = jnp.concatenate([packed, meta], axis=1)
-    got = lax.all_to_all(payload, "patch", split_axis=0, concat_axis=0, tiled=True)
+    got = sent_to_each(payload, "patch", 0, 0)
     body_rows = capacity * 2 * strip_rows
     got_meta = got[:, body_rows:, :]
     visit_count = jnp.sum(got_meta[:, 3, :VISITS], axis=0)

time: 93.3 us -> 89 us (0.954)
  the two profiles are of different devices: /device:TPU:0 before, /device:TPU:13 now
where the time goes in v1:
time: 89 us; the launch traced here: 88.4 us
  other arithmetic  24.8 us (28%)
  matrix products  24.6 us (28%)
  waiting for transfers between devices  14.5 us (16%)
  local copies, waits for them, and re-layouts  14.2 us (16%)
  starting transfers between devices  8.67 us (10%)
  between operations  1.31 us (1%)
    ppermute x7, waiting for transfers between devices, sent_to_each(): lax.ppermute(sent, axis, [(i, (i + step) % size) for i in range(size)])  14.5 us
    dot_general x8, matrix products, place_group(): jnp.einsum('vmwn,vny->vmwy', pixel_block_tile, column_selection, precisio...  11.7 us
    ppermute x7, starting transfers between devices, sent_to_each(): lax.ppermute(sent, axis, [(i, (i + step) % size) for i in range(size)])  8.67 us
    unnamed x39, local copies, waits for them, and re-layouts  6.92 us
    mul x6, other arithmetic, tap_values(): jnp.exp(-offsets * offsets / (2.0 * spread * spread)) / gauss_total * inside  6.87 us
    mul x6, other arithmetic, tap_values(): profile * scaled  6.55 us
    dot_general x8, matrix products, place_group(): jnp.einsum('gri,gkip->krp', row_select, broadened_width, precision=larges...  5.73 us
    dot_general x1, matrix products, convolve_all(): fields = jnp.einsum('nkry,nkyz->nrz', smooth, mixed, precision=mxu_value)  4.08 us
  transfers between devices with their start and end apart: 7, of which 4 were waited for; matrix products, arithmetic and copies ran while one was open for 5% of the time, Pallas kernels for 0%

profile of v1, /device:TPU:13, one launch (start us, length us, event | category | flops | bytes accessed | tf_op | source)
XLA Modules:
  0.0 88.4 jit_solution(4236304657659100527)
XLA Ops:
  0.7 0.6 exponential_reduce_fusion.2
  1.4 0.7 divide_select_fusion.5
  2.0 0.7 fusion.49
  2.7 0.6 exponential_reduce_fusion.1
  3.3 0.7 divide_select_fusion.4
  4.0 0.7 fusion.51
  4.7 0.6 exponential_reduce_fusion
  5.3 0.7 divide_select_fusion.3
  6.0 0.7 fusion.47
  6.7 1.6 %divide_select_fusion.2 = (f32[1,256,276]{1,2,0:T(8,128)}, f32[1,256,276]{1,2,0:T(8,128)}) fusion(f32[]{:T(128)} %exponential_reduce_fusion.2), kind=kLoop, calls=%fused_computation.56 | loop fusion | flops 918528 | bytes 565252 | tf_op jit(solution)/shard_map/mul | solution.py:44
  8.3 1.5 %fusion.29 = f32[1,256,276]{1,2,0:T(8,128)} fusion(f32[]{:T(128)} %exponential_reduce_fusion.2), kind=kLoop, calls=%fused_computation.65 | loop fusion | flops 847872 | bytes 282628 | tf_op jit(solution)/shard_map/mul | solution.py:46
  9.8 1.6 %divide_select_fusion.1 = (f32[1,256,276]{1,2,0:T(8,128)}, f32[1,256,276]{1,2,0:T(8,128)}) fusion(f32[]{:T(128)} %exponential_reduce_fusion.1), kind=kLoop, calls=%fused_computation.55 | loop fusion | flops 918528 | bytes 565252 | tf_op jit(solution)/shard_map/mul | solution.py:44
  11.5 1.5 %fusion.31 = f32[1,256,276]{1,2,0:T(8,128)} fusion(f32[]{:T(128)} %exponential_reduce_fusion.1), kind=kLoop, calls=%fused_computation.67 | loop fusion | flops 847872 | bytes 282628 | tf_op jit(solution)/shard_map/mul | solution.py:46
  13.0 1.6 %divide_select_fusion = (f32[1,256,276]{1,2,0:T(8,128)}, f32[1,256,276]{1,2,0:T(8,128)}) fusion(f32[]{:T(128)} %exponential_reduce_fusion), kind=kLoop, calls=%fused_computation.54 | loop fusion | flops 918528 | bytes 565252 | tf_op jit(solution)/shard_map/mul | solution.py:44
  14.6 1.5 %fusion.27 = f32[1,256,276]{1,2,0:T(8,128)} fusion(f32[]{:T(128)} %exponential_reduce_fusion), kind=kLoop, calls=%fused_computation.63 | loop fusion | flops 847872 | bytes 282628 | tf_op jit(solution)/shard_map/mul | solution.py:46
  17.8 0.4 multiply_add_fusion.1
  18.4 2.7 %multiply_reduce_fusion = f32[2,3,3,128,3,128]{5,3,4,2,1,0:T(8,128)} fusion(f32[2,3,3,3,3,128]{5,4,3,2,1,0:T(4,128)S(1)} %pad_maximum_fusion.3, f32[3,3,128,128]{3,2,1,0:T(8,128)S(1)} %pad_maximum_fusion.1), kind=kLoop, calls=%fused_computation.21 | loop fusion | flops 4423680 | bytes 4211712 | tf_op jit(solution)/shard_map/reduce_sum | solution.py:81
  21.2 3.3 %copy.65 = f32[2,3,3,128,3,128]{3,5,4,2,1,0:T(8,128)S(1)} copy(f32[2,3,3,128,3,128]{5,3,4,2,1,0:T(8,128)} %multiply_reduce_fusion) | data formatting | bytes 7077888 | tf_op jit(solution)/shard_map/reduce_sum | solution.py:81
  24.5 1.3 %select_reduce_fusion = (f32[2]{0:T(128)S(1)}, f32[2]{0:T(128)S(1)}, pred[2,256,128]{2,1,0:T(8,128)(4,1)S(1)}) fusion(f32[2,256,128]{2,1,0:T(8,128)} %param.17, s32[2,256,128]{2,1,0:T(8,128)} %param.18), kind=kLoop, calls=%fused_computation.75 | loop fusion | flops 393212 | bytes 589840 | tf_op jit(solution)/shard_map/reduce_sum | solution.py:141
  25.8 0.9 %convert_reduce_fusion.1 = s32[64]{0:T(128)S(1)} fusion(s32[64]{0:T(128)} %bitcast.148), kind=kLoop, calls=%fused_computation.118 | loop fusion | flops 20416 | bytes 512 | tf_op jit(solution)/shard_map/reduce_sum | solution.py:146
  26.7 0.7 multiply_add_fusion.4
  27.6 0.8 copy-done.2
  29.0 0.7 copy-done.9
  29.7 2.2 %fusion.24 = f32[2,128,9,256]{3,1,2,0:T(8,128)S(1)} fusion(f32[9,256,276,1]{1,2,0,3:T(8,128)S(1)} %bitcast.129, f32[2,256,128]{2,1,0:T(8,128)S(1)} %copy-done.9), kind=kOutput, calls=%fused_computation.52 | convolution fusion | flops 976748544 | bytes 5165056 | tf_op jit(solution)/shard_map/krj,njx->nkrx/dot_general | solution.py:68
  31.9 4.1 %fusion.18 = f32[2,256,384]{2,1,0:T(8,128)S(1)} fusion(f32[2,9,128,384]{2,3,1,0:T(8,128)S(1)} %bitcast.128, f32[2,128,9,256]{3,1,2,0:T(8,128)S(1)} %fusion.24), kind=kOutput, calls=%fused_computation.33 | convolution fusion | flops 1358954496 | bytes 6684672 | tf_op jit(solution)/shard_map/nkry,nkyz->nrz/dot_general | solution.py:83
  36.2 0.7 fusion.21
  37.2 0.4 copy-done.13
  38.2 0.3 scatter.11
  38.4 0.4 scatter.14
  39.0 1.3 %collective-permute-start = (f32[1,264,128]{2,1,0:T(8,128)S(1)}, f32[1,264,128]{2,1,0:T(8,128)}, u32[]{:S(2)}, u32[]{:S(2)}) collective-permute-start(f32[1,264,128]{2,1,0:T(8,128)S(1)} %get-tuple-element.172), channel_id=1, source_target_pairs={{0,4},{4,8},{8,12},{12,16},{16,20},{20,24},{24,28},{28,0},{1,5},{5... | collective-permute-start | bytes 405512 | tf_op jit(solution)/shard_map/ppermute | solution.py:33
  40.3 1.3 %collective-permute-start.1 = (f32[1,264,128]{2,1,0:T(8,128)S(1)}, f32[1,264,128]{2,1,0:T(8,128)}, u32[]{:S(2)}, u32[]{:S(2)}) collective-permute-start(f32[1,264,128]{2,1,0:T(8,128)S(1)} %get-tuple-element.173), channel_id=1, source_target_pairs={{0,8},{4,12},{8,16},{12,20},{16,24},{20,28},{24,0},{28,4},{1,9},{5... | collective-permute-start | bytes 405512 | tf_op jit(solution)/shard_map/ppermute | solution.py:33
  41.6 1.0 %collective-permute-start.2 = (f32[1,264,128]{2,1,0:T(8,128)S(1)}, f32[1,264,128]{2,1,0:T(8,128)}, u32[]{:S(2)}, u32[]{:S(2)}) collective-permute-start(f32[1,264,128]{2,1,0:T(8,128)S(1)} %get-tuple-element.174), channel_id=1, source_target_pairs={{0,12},{4,16},{8,20},{12,24},{16,28},{20,0},{24,4},{28,8},{1,13},{... | collective-permute-start | bytes 405512 | tf_op jit(solution)/shard_map/ppermute | solution.py:33
  42.5 1.3 %collective-permute-start.3 = (f32[1,264,128]{2,1,0:T(8,128)S(1)}, f32[1,264,128]{2,1,0:T(8,128)}, u32[]{:S(2)}, u32[]{:S(2)}) collective-permute-start(f32[1,264,128]{2,1,0:T(8,128)S(1)} %get-tuple-element.175), channel_id=1, source_target_pairs={{0,16},{4,20},{8,24},{12,28},{16,0},{20,4},{24,8},{28,12},{1,17},{... | collective-permute-start | bytes 405512 | tf_op jit(solution)/shard_map/ppermute | solution.py:33
  43.9 1.0 %collective-permute-start.4 = (f32[1,264,128]{2,1,0:T(8,128)S(1)}, f32[1,264,128]{2,1,0:T(8,128)}, u32[]{:S(2)}, u32[]{:S(2)}) collective-permute-start(f32[1,264,128]{2,1,0:T(8,128)S(1)} %get-tuple-element.176), channel_id=1, source_target_pairs={{0,20},{4,24},{8,28},{12,0},{16,4},{20,8},{24,12},{28,16},{1,21},{... | collective-permute-start | bytes 405512 | tf_op jit(solution)/shard_map/ppermute | solution.py:33
  45.0 1.3 %collective-permute-start.5 = (f32[1,264,128]{2,1,0:T(8,128)S(1)}, f32[1,264,128]{2,1,0:T(8,128)S(1)}, u32[]{:S(2)}, u32[]{:S(2)}) collective-permute-start(f32[1,264,128]{2,1,0:T(8,128)S(1)} %fusion.45), channel_id=1, source_target_pairs={{0,24},{4,28},{8,0},{12,4},{16,8},{20,12},{24,16},{28,20},{1,25},{... | collective-permute-start | bytes 405512 | tf_op jit(solution)/shard_map/ppermute | solution.py:33
  46.3 0.9 %bitcast_dynamic-update-slice_fusion.5 = f32[8,1,264,128]{3,2,0,1:T(8,128)S(1)} fusion(f32[8,1,264,128]{3,2,0,1:T(8,128)S(1)} %fusion.39, f32[1,264,128]{2,1,0:T(8,128)} %collective-permute-done), kind=kLoop, calls=%fused_computation.95 | loop fusion | bytes 270336
  47.2 1.5 %collective-permute-start.6 = (f32[1,264,128]{2,1,0:T(8,128)S(1)}, f32[1,264,128]{2,1,0:T(8,128)S(1)}, u32[]{:S(2)}, u32[]{:S(2)}) collective-permute-start(f32[1,264,128]{2,1,0:T(8,128)S(1)} %get-tuple-element.171), channel_id=1, source_target_pairs={{0,28},{4,0},{8,4},{12,8},{16,12},{20,16},{24,20},{28,24},{1,29},{... | collective-permute-start | bytes 405512 | tf_op jit(solution)/shard_map/ppermute | solution.py:33
  48.7 0.9 %bitcast_dynamic-update-slice_fusion.4 = f32[8,1,264,128]{3,2,0,1:T(8,128)S(1)} fusion(f32[8,1,264,128]{3,2,0,1:T(8,128)S(1)} %bitcast_dynamic-update-slice_fusion.5, f32[1,264,128]{2,1,0:T(8,128)} %collective-permute-done.1), kind=kLoop, calls=%fused_computation.94 | loop fusion | bytes 270336
  49.6 10.3 %collective-permute-done.2 = f32[1,264,128]{2,1,0:T(8,128)} collective-permute-done((f32[1,264,128]{2,1,0:T(8,128)S(1)}, f32[1,264,128]{2,1,0:T(8,128)}, u32[]{:S(2)}, u32[]{:S(2)}) %collective-permute-start.2) | collective-permute-done | bytes 135200 | tf_op jit(solution)/shard_map/ppermute | solution.py:33
  59.9 0.9 %bitcast_dynamic-update-slice_fusion.3 = f32[8,1,264,128]{3,2,0,1:T(8,128)S(1)} fusion(f32[8,1,264,128]{3,2,0,1:T(8,128)S(1)} %bitcast_dynamic-update-slice_fusion.4, f32[1,264,128]{2,1,0:T(8,128)} %collective-permute-done.2), kind=kLoop, calls=%fused_computation.93 | loop fusion | bytes 270336
  60.8 2.0 %collective-permute-done.3 = f32[1,264,128]{2,1,0:T(8,128)} collective-permute-done((f32[1,264,128]{2,1,0:T(8,128)S(1)}, f32[1,264,128]{2,1,0:T(8,128)}, u32[]{:S(2)}, u32[]{:S(2)}) %collective-permute-start.3) | collective-permute-done | bytes 135200 | tf_op jit(solution)/shard_map/ppermute | solution.py:33
  62.8 0.9 %bitcast_dynamic-update-slice_fusion.2 = f32[8,1,264,128]{3,2,0,1:T(8,128)S(1)} fusion(f32[8,1,264,128]{3,2,0,1:T(8,128)S(1)} %bitcast_dynamic-update-slice_fusion.3, f32[1,264,128]{2,1,0:T(8,128)} %collective-permute-done.3), kind=kLoop, calls=%fused_computation.92 | loop fusion | bytes 270336
  63.8 0.9 %bitcast_dynamic-update-slice_fusion.1 = f32[8,1,264,128]{3,2,0,1:T(8,128)S(1)} fusion(f32[8,1,264,128]{3,2,0,1:T(8,128)S(1)} %bitcast_dynamic-update-slice_fusion.2, f32[1,264,128]{2,1,0:T(8,128)} %collective-permute-done.4), kind=kLoop, calls=%fused_computation.91 | loop fusion | bytes 270336
  64.7 1.0 %collective-permute-done.5 = f32[1,264,128]{2,1,0:T(8,128)S(1)} collective-permute-done((f32[1,264,128]{2,1,0:T(8,128)S(1)}, f32[1,264,128]{2,1,0:T(8,128)S(1)}, u32[]{:S(2)}, u32[]{:S(2)}) %collective-permute-start.5) | collective-permute-done | bytes 135200 | tf_op jit(solution)/shard_map/ppermute | solution.py:33
  65.7 1.2 %collective-permute-done.6 = f32[1,264,128]{2,1,0:T(8,128)S(1)} collective-permute-done((f32[1,264,128]{2,1,0:T(8,128)S(1)}, f32[1,264,128]{2,1,0:T(8,128)S(1)}, u32[]{:S(2)}, u32[]{:S(2)}) %collective-permute-start.6) | collective-permute-done | bytes 135200 | tf_op jit(solution)/shard_map/ppermute | solution.py:33
  66.9 0.6 gather_fusion
  68.2 19.2 %while.16 = (s32[]{:T(128)}, f32[2,128,512]{1,2,0:T(8,128)S(1)}, f32[8,16,2,8,128]{4,3,2,1,0:T(8,128)S(1)}, s32[8,16,2]{1,0,2:T(8,128)S(1)}, s32[]{:T(128)}, /*index=5*/s32[]{:T(128)}) while((s32[]{:T(128)}, f32[2,128,512]{1,2,0:T(8,128)S(1)}, f32[8,16,2,8,128]{4,3,2,1,0:T(8,128)S(1)}, s32[8,16,2]{1,0,2:T(8,128)S(1)}, ...), condition=%wide.region_13.14_spmd.clone.clone, body=%wide.region_12.13_spmd.clone.clone.sunk | while | flops 403982464 | bytes 2279127 | solution.py:124
  68.3 1.5 %fusion.82 = f32[16,2,8,512]{3,2,1,0:T(8,128)S(1)} fusion(s32[16,128]{1,0:T(8,128)S(1)} %iota_add_fusion.4, f32[8,16,2,8,128]{4,3,2,1,0:T(8,128)S(1)} %get-tuple-element.244, s32[]{:T(128)} %get-tuple-element.236), kind=kOutput, calls=%fused_computation.6.clone.1 | convolution fusion | flops 202375168 | bytes 663556 | tf_op jit(solution)/shard_map/while/body/eval_jaxpr/vmwn,vny->vmwy/dot_general | solution.py:114
  69.8 0.7 fusion.84
  70.7 1.5 %fusion.82 = f32[16,2,8,512]{3,2,1,0:T(8,128)S(1)} fusion(s32[16,128]{1,0:T(8,128)S(1)} %iota_add_fusion.4, f32[8,16,2,8,128]{4,3,2,1,0:T(8,128)S(1)} %get-tuple-element.244, s32[]{:T(128)} %get-tuple-element.236), kind=kOutput, calls=%fused_computation.6.clone.1 | convolution fusion | flops 202375168 | bytes 663556 | tf_op jit(solution)/shard_map/while/body/eval_jaxpr/vmwn,vny->vmwy/dot_general | solution.py:114
  72.3 0.7 fusion.84
  73.1 1.5 %fusion.82 = f32[16,2,8,512]{3,2,1,0:T(8,128)S(1)} fusion(s32[16,128]{1,0:T(8,128)S(1)} %iota_add_fusion.4, f32[8,16,2,8,128]{4,3,2,1,0:T(8,128)S(1)} %get-tuple-element.244, s32[]{:T(128)} %get-tuple-element.236), kind=kOutput, calls=%fused_computation.6.clone.1 | convolution fusion | flops 202375168 | bytes 663556 | tf_op jit(solution)/shard_map/while/body/eval_jaxpr/vmwn,vny->vmwy/dot_general | solution.py:114
  74.7 0.7 fusion.84
  75.5 1.5 %fusion.82 = f32[16,2,8,512]{3,2,1,0:T(8,128)S(1)} fusion(s32[16,128]{1,0:T(8,128)S(1)} %iota_add_fusion.4, f32[8,16,2,8,128]{4,3,2,1,0:T(8,128)S(1)} %get-tuple-element.244, s32[]{:T(128)} %get-tuple-element.236), kind=kOutput, calls=%fused_computation.6.clone.1 | convolution fusion | flops 202375168 | bytes 663556 | tf_op jit(solution)/shard_map/while/body/eval_jaxpr/vmwn,vny->vmwy/dot_general | solution.py:114
  77.1 0.7 fusion.84
  77.9 1.5 %fusion.82 = f32[16,2,8,512]{3,2,1,0:T(8,128)S(1)} fusion(s32[16,128]{1,0:T(8,128)S(1)} %iota_add_fusion.4, f32[8,16,2,8,128]{4,3,2,1,0:T(8,128)S(1)} %get-tuple-element.244, s32[]{:T(128)} %get-tuple-element.236), kind=kOutput, calls=%fused_computation.6.clone.1 | convolution fusion | flops 202375168 | bytes 663556 | tf_op jit(solution)/shard_map/while/body/eval_jaxpr/vmwn,vny->vmwy/dot_general | solution.py:114
  79.5 0.7 fusion.84
  80.3 1.5 %fusion.82 = f32[16,2,8,512]{3,2,1,0:T(8,128)S(1)} fusion(s32[16,128]{1,0:T(8,128)S(1)} %iota_add_fusion.4, f32[8,16,2,8,128]{4,3,2,1,0:T(8,128)S(1)} %get-tuple-element.244, s32[]{:T(128)} %get-tuple-element.236), kind=kOutput, calls=%fused_computation.6.clone.1 | convolution fusion | flops 202375168 | bytes 663556 | tf_op jit(solution)/shard_map/while/body/eval_jaxpr/vmwn,vny->vmwy/dot_general | solution.py:114
  81.9 0.7 fusion.84
  82.7 1.5 %fusion.82 = f32[16,2,8,512]{3,2,1,0:T(8,128)S(1)} fusion(s32[16,128]{1,0:T(8,128)S(1)} %iota_add_fusion.4, f32[8,16,2,8,128]{4,3,2,1,0:T(8,128)S(1)} %get-tuple-element.244, s32[]{:T(128)} %get-tuple-element.236), kind=kOutput, calls=%fused_computation.6.clone.1 | convolution fusion | flops 202375168 | bytes 663556 | tf_op jit(solution)/shard_map/while/body/eval_jaxpr/vmwn,vny->vmwy/dot_general | solution.py:114
  84.3 0.7 fusion.84
  85.1 1.5 %fusion.82 = f32[16,2,8,512]{3,2,1,0:T(8,128)S(1)} fusion(s32[16,128]{1,0:T(8,128)S(1)} %iota_add_fusion.4, f32[8,16,2,8,128]{4,3,2,1,0:T(8,128)S(1)} %get-tuple-element.244, s32[]{:T(128)} %get-tuple-element.236), kind=kOutput, calls=%fused_computation.6.clone.1 | convolution fusion | flops 202375168 | bytes 663556 | tf_op jit(solution)/shard_map/while/body/eval_jaxpr/vmwn,vny->vmwy/dot_general | solution.py:114
  86.7 0.7 fusion.84
  87.6 0.8 slice_divide_fusion
  (130 shorter events, 5.8 us)
Async XLA Ops:
  8.3 7.7 %copy-start.10 = (f32[2,27,6]{1,0,2:T(2,128)S(1)}, f32[2,27,6]{1,0,2:T(2,128)}, u32[]{:S(2)}) copy-start(f32[2,27,6]{1,0,2:T(2,128)} %param.19) | copy-start | bytes 3892
  24.5 2.9 %copy-start = (f32[1,256,276]{1,2,0:T(8,128)S(1)}, f32[1,256,276]{1,2,0:T(8,128)}, u32[]{:S(2)}) copy-start(f32[1,256,276]{1,2,0:T(8,128)} %fusion.29) | copy-start | bytes 847876
  24.5 2.9 %copy-start.3 = (f32[1,256,276]{1,2,0:T(8,128)S(1)}, f32[1,256,276]{1,2,0:T(8,128)}, u32[]{:S(2)}) copy-start(f32[1,256,276]{1,2,0:T(8,128)} %get-tuple-element.195) | copy-start | bytes 847876
  24.5 2.9 %copy-start.4 = (f32[1,256,276]{1,2,0:T(8,128)S(1)}, f32[1,256,276]{1,2,0:T(8,128)}, u32[]{:S(2)}) copy-start(f32[1,256,276]{1,2,0:T(8,128)} %get-tuple-element.196) | copy-start | bytes 847876
  25.8 1.8 %copy-start.1 = (f32[1,256,276]{1,2,0:T(8,128)S(1)}, f32[1,256,276]{1,2,0:T(8,128)}, u32[]{:S(2)}) copy-start(f32[1,256,276]{1,2,0:T(8,128)} %fusion.31) | copy-start | bytes 847876
  25.8 1.8 %copy-start.5 = (f32[1,256,276]{1,2,0:T(8,128)S(1)}, f32[1,256,276]{1,2,0:T(8,128)}, u32[]{:S(2)}) copy-start(f32[1,256,276]{1,2,0:T(8,128)} %get-tuple-element.191) | copy-start | bytes 847876
  25.8 1.8 %copy-start.6 = (f32[1,256,276]{1,2,0:T(8,128)S(1)}, f32[1,256,276]{1,2,0:T(8,128)}, u32[]{:S(2)}) copy-start(f32[1,256,276]{1,2,0:T(8,128)} %get-tuple-element.192) | copy-start | bytes 847876
  27.4 8.8 %copy-start.11 = (s32[64]{0:T(128)}, s32[64]{0:T(128)S(1)}, u32[]{:S(2)}) copy-start(s32[64]{0:T(128)S(1)} %multiply_add_fusion.4) | copy-start | bytes 772
  27.5 1.0 %copy-start.2 = (f32[1,256,276]{1,2,0:T(8,128)S(1)}, f32[1,256,276]{1,2,0:T(8,128)}, u32[]{:S(2)}) copy-start(f32[1,256,276]{1,2,0:T(8,128)} %fusion.27) | copy-start | bytes 847876
  27.5 1.0 %copy-start.7 = (f32[1,256,276]{1,2,0:T(8,128)S(1)}, f32[1,256,276]{1,2,0:T(8,128)}, u32[]{:S(2)}) copy-start(f32[1,256,276]{1,2,0:T(8,128)} %get-tuple-element.187) | copy-start | bytes 847876
  27.5 1.1 %copy-start.8 = (f32[1,256,276]{1,2,0:T(8,128)S(1)}, f32[1,256,276]{1,2,0:T(8,128)}, u32[]{:S(2)}) copy-start(f32[1,256,276]{1,2,0:T(8,128)} %get-tuple-element.188) | copy-start | bytes 847876
  28.7 1.0 %copy-start.9 = (f32[2,256,128]{2,1,0:T(8,128)S(1)}, f32[2,256,128]{2,1,0:T(8,128)}, u32[]{:S(2)}) copy-start(f32[2,256,128]{2,1,0:T(8,128)} %param.16) | copy-start | bytes 786436
  36.9 0.7 copy-start.13
  37.0 0.8 copy-start.12
  37.0 0.8 copy-start.14
  37.0 0.8 copy-start.15
  39.0 6.0 %collective-permute-start = (f32[1,264,128]{2,1,0:T(8,128)S(1)}, f32[1,264,128]{2,1,0:T(8,128)}, u32[]{:S(2)}, u32[]{:S(2)}) collective-permute-start(f32[1,264,128]{2,1,0:T(8,128)S(1)} %get-tuple-element.172), channel_id=1, source_target_pairs={{0,4},{4,8},{8,12},{12,16},{16,20},{20,24},{24,28},{28,0},{1,5},{5... | collective-permute-start | bytes 405512 | tf_op jit(solution)/shard_map/ppermute | solution.py:33
  40.3 7.0 %collective-permute-start.1 = (f32[1,264,128]{2,1,0:T(8,128)S(1)}, f32[1,264,128]{2,1,0:T(8,128)}, u32[]{:S(2)}, u32[]{:S(2)}) collective-permute-start(f32[1,264,128]{2,1,0:T(8,128)S(1)} %get-tuple-element.173), channel_id=1, source_target_pairs={{0,8},{4,12},{8,16},{12,20},{16,24},{20,28},{24,0},{28,4},{1,9},{5... | collective-permute-start | bytes 405512 | tf_op jit(solution)/shard_map/ppermute | solution.py:33
  41.6 18.4 %collective-permute-start.2 = (f32[1,264,128]{2,1,0:T(8,128)S(1)}, f32[1,264,128]{2,1,0:T(8,128)}, u32[]{:S(2)}, u32[]{:S(2)}) collective-permute-start(f32[1,264,128]{2,1,0:T(8,128)S(1)} %get-tuple-element.174), channel_id=1, source_target_pairs={{0,12},{4,16},{8,20},{12,24},{16,28},{20,0},{24,4},{28,8},{1,13},{... | collective-permute-start | bytes 405512 | tf_op jit(solution)/shard_map/ppermute | solution.py:33
  42.5 20.3 %collective-permute-start.3 = (f32[1,264,128]{2,1,0:T(8,128)S(1)}, f32[1,264,128]{2,1,0:T(8,128)}, u32[]{:S(2)}, u32[]{:S(2)}) collective-permute-start(f32[1,264,128]{2,1,0:T(8,128)S(1)} %get-tuple-element.175), channel_id=1, source_target_pairs={{0,16},{4,20},{8,24},{12,28},{16,0},{20,4},{24,8},{28,12},{1,17},{... | collective-permute-start | bytes 405512 | tf_op jit(solution)/shard_map/ppermute | solution.py:33
  43.9 19.9 %collective-permute-start.4 = (f32[1,264,128]{2,1,0:T(8,128)S(1)}, f32[1,264,128]{2,1,0:T(8,128)}, u32[]{:S(2)}, u32[]{:S(2)}) collective-permute-start(f32[1,264,128]{2,1,0:T(8,128)S(1)} %get-tuple-element.176), channel_id=1, source_target_pairs={{0,20},{4,24},{8,28},{12,0},{16,4},{20,8},{24,12},{28,16},{1,21},{... | collective-permute-start | bytes 405512 | tf_op jit(solution)/shard_map/ppermute | solution.py:33
  45.0 20.7 %collective-permute-start.5 = (f32[1,264,128]{2,1,0:T(8,128)S(1)}, f32[1,264,128]{2,1,0:T(8,128)S(1)}, u32[]{:S(2)}, u32[]{:S(2)}) collective-permute-start(f32[1,264,128]{2,1,0:T(8,128)S(1)} %fusion.45), channel_id=1, source_target_pairs={{0,24},{4,28},{8,0},{12,4},{16,8},{20,12},{24,16},{28,20},{1,25},{... | collective-permute-start | bytes 405512 | tf_op jit(solution)/shard_map/ppermute | solution.py:33
  47.2 19.7 %collective-permute-start.6 = (f32[1,264,128]{2,1,0:T(8,128)S(1)}, f32[1,264,128]{2,1,0:T(8,128)S(1)}, u32[]{:S(2)}, u32[]{:S(2)}) collective-permute-start(f32[1,264,128]{2,1,0:T(8,128)S(1)} %get-tuple-element.171), channel_id=1, source_target_pairs={{0,28},{4,0},{8,4},{12,8},{16,12},{20,16},{24,20},{28,24},{1,29},{... | collective-permute-start | bytes 405512 | tf_op jit(solution)/shard_map/ppermute | solution.py:33
